TPU v7x, 128 devices: a whole 4x4x4 slice. The times are simulated.
128 devices in a mesh: dp: 8 (over x, core), eig: 16 (over y, z).
Axes of the slice: x: 4, y: 4, z: 4, core: 2. Of those that a mesh axis runs over, the one named last changes fastest.
Arguments:
- acts: bfloat16 [4096, 8192], P(('dp', 'eig')), may hold values from -6 to 6
- grads: bfloat16 [4096, 8192], P(('dp', 'eig')), may hold values from -6 to 6
- act_basis: bfloat16 [4096, 8192], P('eig'), may hold values from -0.0625 to 0.0625
- grad_basis: bfloat16 [4096, 8192], P('eig'), may hold values from -0.0625 to 0.0625
- eigenvalues: float32 [4096, 4096], P('eig'), may hold values from 0.05 to 20
- query_grads: bfloat16 [32, 256, 4096], P('dp', None, 'eig'), may hold values from -6 to 6
- query_acts: bfloat16 [32, 256, 4096], P('dp'), may hold values from -6 to 6
- cand_local: int32 [8, 16], P('dp'), may hold values from 0 to 7, as said below
- seq_lengths: int32 [8, 8], P('dp'), may hold values from 1 to 128, 512 in all within a row
Outputs:
- scores: float32 [32, 16], P('dp')
Inputs may be any that keep to these rules, and one draw needn't show every extreme that they name: `cand_local`: entry j of an owner's list names a sequence of dp shard j // 2; the 2 entries of one list that name one shard differ. `seq_lengths`: row d lists the lengths of the 8 sequences packed in order in dp shard d's 512 token rows; they sum to 512.
All inputs are finite; a program needn't handle non-finite values.
Results may differ from a plain program's by a relative error of at most 0.006.
Values may be sent and summed in bfloat16 or wider, within the bound.
No kernel may reach another device: no remote copies, remote signals or barrier semaphores. Data moves between devices by JAX's collectives and lax.ppermute only.
A program may use at most 128 MiB of HBM per device.

v0:
```python
import math
import jax
import jax.numpy as jnp
from jax import lax
from jax.sharding import PartitionSpec as P

DAMPING = 0.1


def shards(
    acts,
    grads,
    act_basis,
    grad_basis,
    eigenvalues,
    query_grads,
    query_acts,
    cand_local,
    seq_lengths,
):
    block_width = act_basis.shape[0]
    queries = query_grads.shape[0]
    full_width = query_acts.shape[2]
    seq_count = seq_lengths.shape[1]
    group_rows = acts.shape[0] * lax.axis_size("eig")
    max_len = 2 * group_rows // seq_count
    pick_lists = lax.all_to_all(cand_local, "dp", split_axis=1, concat_axis=0, tiled=True)
    owners = pick_lists.shape[0]
    per_shard = pick_lists.shape[1]
    lengths = seq_lengths[0]
    offsets = jnp.cumsum(lengths) - lengths
    chosen = (
        pick_lists[:, :, None] == jnp.arange(seq_count, dtype=jnp.int32)[None, None, :]
    ).astype(jnp.int32)
    pick_len = jnp.sum(chosen * lengths[None, None, :], axis=2)
    pick_start = jnp.sum(chosen * offsets[None, None, :], axis=2)
    within = jnp.arange(max_len, dtype=jnp.int32)
    is_live = within[None, None, :] < pick_len[:, :, None]
    row_index = jnp.where(is_live, pick_start[:, :, None] + within[None, None, :], -1).reshape(-1)
    select = (row_index[:, None] == jnp.arange(group_rows, dtype=jnp.int32)[None, :]).astype(
        jnp.bfloat16
    )

    def rotate_and_pack(rows, basis):
        shard_rows = lax.all_gather(rows, "eig", axis=0, tiled=True)
        rotated = jnp.dot(shard_rows, basis.T, preferred_element_type=jnp.float32).astype(
            jnp.bfloat16
        )
        rotated = lax.optimization_barrier(rotated)
        packed = jnp.dot(select, rotated, preferred_element_type=jnp.float32).astype(jnp.bfloat16)
        packed = packed.reshape(owners, per_shard * max_len, block_width)
        return lax.all_to_all(packed, "dp", split_axis=0, concat_axis=0, tiled=True)

    act_narrow = rotate_and_pack(acts, act_basis)
    act_recv = lax.all_gather(act_narrow, "eig", axis=2, tiled=True)
    grad_recv = rotate_and_pack(grads, grad_basis)
    slot_count = owners * per_shard * max_len
    grad_flat = grad_recv.reshape(slot_count, block_width).astype(jnp.float32)
    act_flat = act_recv.reshape(slot_count, full_width)
    damped = eigenvalues + DAMPING
    query_outer = jnp.einsum(
        "qti,qtk->qik", query_grads, query_acts, preferred_element_type=jnp.float32
    )
    precond = (query_outer / damped[None]).astype(jnp.bfloat16)
    precond = lax.optimization_barrier(precond.reshape(queries * block_width, full_width))
    projected = lax.dot_general(
        act_flat, precond, (((1,), (1,)), ((), ())), preferred_element_type=jnp.float32
    )
    projected = lax.optimization_barrier(projected).reshape(slot_count, queries, block_width)
    per_token = jnp.sum(projected * grad_flat[:, None, :], axis=2)
    partial_sums = jnp.sum(per_token.reshape(owners * per_shard, max_len, queries), axis=1).T
    summed = lax.psum(partial_sums, "eig")
    score_scale = 1.0 / (full_width * 4.0 * math.sqrt(query_acts.shape[1]))
    return summed * score_scale


def solution(mesh):
    placed = (
        P(("dp", "eig"), None),
        P(("dp", "eig"), None),
        P("eig", None),
        P("eig", None),
        P("eig", None),
        P("dp", None, "eig"),
        P("dp", None, None),
        P("dp", None),
        P("dp", None),
    )
    return jax.shard_map(
        shards, mesh=mesh, in_specs=placed, out_specs=P("dp", None), check_vma=False
    )
```

profile of v0, /device:TPU:0, one launch (start us, length us, event | category | flops | bytes accessed | tf_op | source)
XLA Modules:
  0.0 363.8 jit_solution(16105542730583716110)
XLA Ops:
  6.5 0.7 all-gather.4.cloned.1.call-update
  8.5 1.3 reduce.3
  10.5 4.4 %all-to-all-start = ((s32[1,8,2]{2,0,1:T(1,128)}), s32[1,8,2]{2,0,1:T(1,128)S(1)}, u32[]{:S(2)}, u32[]{:S(2)}) async-start(s32[1,8,2]{2,0,1:T(1,128)} %bitcast), calls=%async_computation | async-start | bytes 8192 | tf_op jit(solution)/shard_map/all_to_all | solution.py:27
  15.0 0.8 reduce-window.8
  16.5 3.7 %all-to-all-done = s32[1,8,2]{2,0,1:T(1,128)S(1)} async-done(((s32[1,8,2]{2,0,1:T(1,128)}), s32[1,8,2]{2,0,1:T(1,128)S(1)}, u32[]{:S(2)}, u32[]{:S(2)}) %all-to-all-start) | async-done | bytes 96 | tf_op jit(solution)/shard_map/all_to_all | solution.py:27
  20.3 0.9 select_reduce_fusion.1
  21.4 61.6 %all-gather.4.cloned.1.call-done = bf16[512,8192]{1,0:T(8,128)(2,1)} async-done(((bf16[32,8192]{1,0:T(8,128)(2,1)}), bf16[512,8192]{1,0:T(8,128)(2,1)}) %all-gather.4.cloned.1.call-update) | async-done | bytes 8388624 | tf_op jit(solution)/shard_map/all_gather | solution.py:45
  83.0 6.9 %convolution_convert_fusion.1 = bf16[512,256]{1,0:T(8,128)(2,1)S(1)} fusion(bf16[512,8192]{1,0:T(8,128)(2,1)} %all-gather.4.cloned.1.call-done, bf16[256,8192]{1,0:T(8,128)(2,1)} %param.11), kind=kOutput, calls=%fused_computation.11 | convolution fusion | flops 2147614720 | bytes 12845056 | tf_op jit(solution)/shard_map/dot_general | solution.py:46
  89.9 1.1 fusion.2
  91.0 20.1 %all_to_all.23 = bf16[8,256,256]{2,1,0:T(8,128)(2,1)} all-to-all(bf16[8,256,256]{2,1,0:T(8,128)(2,1)S(1)} %bitcast.28), channel_id=1, replica_groups=mesh['dp'=8,'eig'=16] {'dp'}, dimensions={0} | all-to-all | bytes 2097152 | tf_op jit(solution)/shard_map/all_to_all | solution.py:52
  111.2 4.8 %broadcast_add_fusion = f32[256,4096]{1,0:T(8,128)} fusion(f32[256,4096]{1,0:T(8,128)} %param.13), kind=kLoop, calls=%fused_computation.7 | loop fusion | flops 1048576 | bytes 8388608 | tf_op jit(solution)/shard_map/add | solution.py:60
  115.9 39.8 %all-gather.8.cloned.1.call-done = bf16[512,8192]{1,0:T(8,128)(2,1)} async-done(((bf16[32,8192]{1,0:T(8,128)(2,1)}), bf16[512,8192]{1,0:T(8,128)(2,1)}) %all-gather.8.cloned.1.call-update) | async-done | bytes 8388624 | tf_op jit(solution)/shard_map/all_gather | solution.py:45
  155.7 6.9 %convolution_convert_fusion = bf16[512,256]{1,0:T(8,128)(2,1)S(1)} fusion(bf16[512,8192]{1,0:T(8,128)(2,1)} %all-gather.8.cloned.1.call-done, bf16[256,8192]{1,0:T(8,128)(2,1)} %param.12), kind=kOutput, calls=%fused_computation.10 | convolution fusion | flops 2147614720 | bytes 12845056 | tf_op jit(solution)/shard_map/dot_general | solution.py:46
  162.6 1.9 fusion.3
  164.5 4.3 %all-to-all-start.2 = ((bf16[8,256,256]{2,1,0:T(8,128)(2,1)}), bf16[8,256,256]{2,1,0:T(8,128)(2,1)S(1)}, u32[]{:S(2)}, u32[]{:S(2)}) async-start(bf16[8,256,256]{2,1,0:T(8,128)(2,1)} %bitcast.9), calls=%async_computation.2 | async-start | bytes 2097152 | tf_op jit(solution)/shard_map/all_to_all | solution.py:52
  168.7 9.2 %divide_convert_fusion = bf16[4,256,4096]{2,1,0:T(8,128)(2,1)} fusion(f32[256,4096]{1,0:T(8,128)} %broadcast_add_fusion, bf16[4,256,256]{2,1,0:T(8,128)(2,1)S(1)} %copy-done, bf16[4,256,4096]{2,1,0:T(8,128)(2,1)} %param.15), kind=kOutput, calls=%fused_computation | convolution fusion | flops 2155872256 | bytes 21495808 | tf_op jit(solution)/shard_map/qti,qtk->qik/dot_general | solution.py:61
  177.9 6.7 %all-to-all-done.2 = bf16[8,256,256]{2,1,0:T(8,128)(2,1)S(1)} async-done(((bf16[8,256,256]{2,1,0:T(8,128)(2,1)}), bf16[8,256,256]{2,1,0:T(8,128)(2,1)S(1)}, u32[]{:S(2)}, u32[]{:S(2)}) %all-to-all-start.2) | async-done | bytes 1048608 | tf_op jit(solution)/shard_map/all_to_all | solution.py:52
  184.7 1.1 copy-done.2
  185.7 1.4 convert.1
  187.1 90.2 %all-gather.6.cloned.1.call-done = bf16[8,256,4096]{2,1,0:T(8,128)(2,1)} async-done(((bf16[8,256,256]{2,1,0:T(8,128)(2,1)}), bf16[8,256,4096]{2,1,0:T(8,128)(2,1)}) %all-gather.6.cloned.1.call-update) | async-done | bytes 16777232 | tf_op jit(solution)/shard_map/all_gather | solution.py:55
  277.4 24.1 %fusion.6 = f32[2048,1024]{1,0:T(8,128)} fusion(bf16[2048,4096]{1,0:T(8,128)(2,1)} %bitcast.35, bf16[1024,4096]{1,0:T(8,128)(2,1)} %bitcast.36), kind=kOutput, calls=%fused_computation.19 | convolution fusion | flops 17179869184 | bytes 33554432 | tf_op jit(solution)/shard_map/dot_general | solution.py:66
  301.5 10.6 %reshape.106 = f32[2048,4,256]{2,1,0:T(4,128)} reshape(f32[2048,1024]{1,0:T(8,128)} %fusion.6) | data formatting | bytes 16777216 | tf_op jit(solution)/shard_map/reshape | solution.py:69
  312.1 6.3 %multiply_reduce_fusion = f32[2048,4]{1,0:T(8,128)S(1)} fusion(f32[2048,4,256]{2,1,0:T(4,128)} %reshape.106, f32[2048,256]{1,0:T(8,128)S(1)} %convert.1), kind=kLoop, calls=%fused_computation.1 | loop fusion | flops 4186112 | bytes 10518528 | tf_op jit(solution)/shard_map/reduce_sum | solution.py:70
  318.6 38.1 %psum.7 = f32[4,16]{1,0:T(4,128)S(1)} all-reduce(f32[4,16]{1,0:T(4,128)S(1)} %bitcast.29), channel_id=1, replica_groups=mesh['dp'=8,'eig'=16] {'eig'}, use_global_device_ids=true, to_apply=%region_5.6 | all-reduce | flops 64 | bytes 512 | tf_op jit(solution)/shard_map/psum | solution.py:72
  (20 shorter events, 3.7 us)
Async XLA Ops:
  6.5 162.2 %copy-start = (bf16[4,256,256]{2,1,0:T(8,128)(2,1)S(1)}, bf16[4,256,256]{2,1,0:T(8,128)(2,1)}, u32[]{:S(2)}) copy-start(bf16[4,256,256]{2,1,0:T(8,128)(2,1)} %param.14) | copy-start | bytes 1572868
  6.5 76.4 %all-gather.4.cloned.1.call-start = ((), (), s32[]{:S(2)}) async-start(), calls=%async_computation.3 | async-start | bytes 8912896 | tf_op jit(solution)/shard_map/all_gather | solution.py:45
  7.3 148.4 %all-gather.8.cloned.1.call-start = ((), (), s32[]{:S(2)}) async-start(), calls=%async_computation.5 | async-start | bytes 8912896 | tf_op jit(solution)/shard_map/all_gather | solution.py:45
  10.5 9.7 %all-to-all-start = ((s32[1,8,2]{2,0,1:T(1,128)}), s32[1,8,2]{2,0,1:T(1,128)S(1)}, u32[]{:S(2)}, u32[]{:S(2)}) async-start(s32[1,8,2]{2,0,1:T(1,128)} %bitcast), calls=%async_computation | async-start | bytes 8192 | tf_op jit(solution)/shard_map/all_to_all | solution.py:27
  14.9 262.5 %all-gather.6.cloned.1.call-start = ((), (), s32[]{:S(2)}) async-start(), calls=%async_computation.4 | async-start | bytes 17825792 | tf_op jit(solution)/shard_map/all_gather | solution.py:55
  164.5 20.2 %all-to-all-start.2 = ((bf16[8,256,256]{2,1,0:T(8,128)(2,1)}), bf16[8,256,256]{2,1,0:T(8,128)(2,1)S(1)}, u32[]{:S(2)}, u32[]{:S(2)}) async-start(bf16[8,256,256]{2,1,0:T(8,128)(2,1)} %bitcast.9), calls=%async_computation.2 | async-start | bytes 2097152 | tf_op jit(solution)/shard_map/all_to_all | solution.py:52
  184.7 1.1 copy-start.2
  301.5 55.8 %copy-start.1 = (bf16[4,256,256]{2,1,0:T(8,128)(2,1)S(1)}, bf16[4,256,256]{2,1,0:T(8,128)(2,1)}, u32[]{:S(2)}) copy-start(bf16[4,256,256]{2,1,0:T(8,128)(2,1)} %param.14) | copy-start | bytes 1572868
Sparse Core Ops, SparseCore 0:
  9.5 73.4 all-gather.3
  85.1 70.4 all-gather.7
  157.8 119.5 all-gather.5
where the time goes:
time: 364 us
  waiting for transfers between devices  203 us (56%)
  blocking collectives  58.3 us (16%)
  matrix products  50.1 us (14%)
  other arithmetic  16.9 us (5%)
  local copies, waits for them, and re-layouts  13.2 us (4%)
  between operations  13.2 us (4%)
  starting transfers between devices  8.75 us (2%)
    all_gather x2, waiting for transfers between devices, rotate_and_pack(): shard_rows = lax.all_gather(rows, 'eig', axis=0, tiled=True)  101 us
    all_gather x1, waiting for transfers between devices, shards(): act_recv = lax.all_gather(act_narrow, 'eig', axis=2, tiled=True)  90.2 us
    psum x1, blocking collectives, shards(): summed = lax.psum(partial_sums, 'eig')  38.1 us
    dot_general x1, matrix products, shards(): lax.dot_general(act_flat, precond, (((1,), (1,)), ((), ())), preferred_el...  24.1 us
    all_to_all x1, blocking collectives, rotate_and_pack(): return lax.all_to_all(packed, 'dp', split_axis=0, concat_axis=0, tiled=True)  20.1 us
    dot_general x2, matrix products, rotate_and_pack(): jnp.dot(shard_rows, basis.T, preferred_element_type=jnp.float32)  13.9 us
    reshape x1, local copies, waits for them, and re-layouts, shards(): lax.optimization_barrier(projected)  10.6 us
    dot_general x1, matrix products, shards(): jnp.einsum('qti,qtk->qik', query_grads, query_acts, preferred_element_typ...  9.21 us
  transfers between devices with their start and end apart: 5, of which 5 were waited for; matrix products, arithmetic and copies ran while one was open for 10% of the time, Pallas kernels for 0%

commit v1 on v0

--- a/solution.py
+++ b/solution.py
@@ -69,7 +69,7 @@
     projected = lax.optimization_barrier(projected).reshape(slot_count, queries, block_width)
     per_token = jnp.sum(projected * grad_flat[:, None, :], axis=2)
     partial_sums = jnp.sum(per_token.reshape(owners * per_shard, max_len, queries), axis=1).T
-    summed = lax.psum(partial_sums, "eig")
+    summed = jnp.sum(lax.all_gather(partial_sums, "eig"), axis=0)
     score_scale = 1.0 / (full_width * 4.0 * math.sqrt(query_acts.shape[1]))
     return summed * score_scale
 

time: 364 us -> 349 us (0.959)
  blocking collectives: 58.3 us -> 42.9 us
    psum x1 -> x0, blocking collectives: 38.1 us -> none  [shards(): summed = lax.psum(partial_sums, 'eig')]
    all_gather x0 -> x1, blocking collectives: none -> 22.7 us  [shards(): summed = jnp.sum(lax.all_gather(partial_sums, 'eig'), axis=0)]
  transfers between devices with their start and end apart: 5 -> 5, of which waited for: 5 -> 5; matrix products, arithmetic and copies ran while one was open for 10% -> 11% of each run, Pallas kernels for 0% -> 0%
where the time goes in v1:
time: 349 us; the launch traced here: 348 us
  waiting for transfers between devices  203 us (58%)
  matrix products  50.1 us (14%)
  blocking collectives  42.9 us (12%)
  other arithmetic  16.9 us (5%)
  local copies, waits for them, and re-layouts  13.2 us (4%)
  between operations  13.2 us (4%)
  starting transfers between devices  8.75 us (3%)
    all_gather x2, waiting for transfers between devices, rotate_and_pack(): shard_rows = lax.all_gather(rows, 'eig', axis=0, tiled=True)  101 us
    all_gather x1, waiting for transfers between devices, shards(): act_recv = lax.all_gather(act_narrow, 'eig', axis=2, tiled=True)  90.2 us
    dot_general x1, matrix products, shards(): lax.dot_general(act_flat, precond, (((1,), (1,)), ((), ())), preferred_el...  24.1 us
    all_gather x1, blocking collectives, shards(): summed = jnp.sum(lax.all_gather(partial_sums, 'eig'), axis=0)  22.7 us
    all_to_all x1, blocking collectives, rotate_and_pack(): return lax.all_to_all(packed, 'dp', split_axis=0, concat_axis=0, tiled=True)  20.1 us
    dot_general x2, matrix products, rotate_and_pack(): jnp.dot(shard_rows, basis.T, preferred_element_type=jnp.float32)  13.9 us
    reshape x1, local copies, waits for them, and re-layouts, shards(): lax.optimization_barrier(projected)  10.6 us
    dot_general x1, matrix products, shards(): jnp.einsum('qti,qtk->qik', query_grads, query_acts, preferred_element_typ...  9.21 us
  transfers between devices with their start and end apart: 5, of which 5 were waited for; matrix products, arithmetic and copies ran while one was open for 11% of the time, Pallas kernels for 0%

profile of v1, /device:TPU:0, one launch (start us, length us, event | category | flops | bytes accessed | tf_op | source)
XLA Modules:
  0.0 348.4 jit_solution(9284170612990531727)
XLA Ops:
  6.5 0.7 all-gather.6.cloned.1.call-update
  8.5 1.3 reduce.4
  10.5 4.4 %all-to-all-start = ((s32[1,8,2]{2,0,1:T(1,128)}), s32[1,8,2]{2,0,1:T(1,128)S(1)}, u32[]{:S(2)}, u32[]{:S(2)}) async-start(s32[1,8,2]{2,0,1:T(1,128)} %bitcast), calls=%async_computation | async-start | bytes 8192 | tf_op jit(solution)/shard_map/all_to_all | solution.py:27
  15.0 0.8 reduce-window.8
  16.5 3.7 %all-to-all-done = s32[1,8,2]{2,0,1:T(1,128)S(1)} async-done(((s32[1,8,2]{2,0,1:T(1,128)}), s32[1,8,2]{2,0,1:T(1,128)S(1)}, u32[]{:S(2)}, u32[]{:S(2)}) %all-to-all-start) | async-done | bytes 96 | tf_op jit(solution)/shard_map/all_to_all | solution.py:27
  20.3 0.9 select_reduce_fusion.1
  21.4 61.6 %all-gather.6.cloned.1.call-done = bf16[512,8192]{1,0:T(8,128)(2,1)} async-done(((bf16[32,8192]{1,0:T(8,128)(2,1)}), bf16[512,8192]{1,0:T(8,128)(2,1)}) %all-gather.6.cloned.1.call-update) | async-done | bytes 8388624 | tf_op jit(solution)/shard_map/all_gather | solution.py:45
  83.0 6.9 %convolution_convert_fusion.1 = bf16[512,256]{1,0:T(8,128)(2,1)S(1)} fusion(bf16[512,8192]{1,0:T(8,128)(2,1)} %all-gather.6.cloned.1.call-done, bf16[256,8192]{1,0:T(8,128)(2,1)} %param.11), kind=kOutput, calls=%fused_computation.11 | convolution fusion | flops 2147614720 | bytes 12845056 | tf_op jit(solution)/shard_map/dot_general | solution.py:46
  89.9 1.1 fusion.2
  91.0 20.1 %all_to_all.23 = bf16[8,256,256]{2,1,0:T(8,128)(2,1)} all-to-all(bf16[8,256,256]{2,1,0:T(8,128)(2,1)S(1)} %bitcast.30), channel_id=1, replica_groups=mesh['dp'=8,'eig'=16] {'dp'}, dimensions={0} | all-to-all | bytes 2097152 | tf_op jit(solution)/shard_map/all_to_all | solution.py:52
  111.2 4.8 %broadcast_add_fusion = f32[256,4096]{1,0:T(8,128)} fusion(f32[256,4096]{1,0:T(8,128)} %param.13), kind=kLoop, calls=%fused_computation.7 | loop fusion | flops 1048576 | bytes 8388608 | tf_op jit(solution)/shard_map/add | solution.py:60
  115.9 39.8 %all-gather.10.cloned.1.call-done = bf16[512,8192]{1,0:T(8,128)(2,1)} async-done(((bf16[32,8192]{1,0:T(8,128)(2,1)}), bf16[512,8192]{1,0:T(8,128)(2,1)}) %all-gather.10.cloned.1.call-update) | async-done | bytes 8388624 | tf_op jit(solution)/shard_map/all_gather | solution.py:45
  155.7 6.9 %convolution_convert_fusion = bf16[512,256]{1,0:T(8,128)(2,1)S(1)} fusion(bf16[512,8192]{1,0:T(8,128)(2,1)} %all-gather.10.cloned.1.call-done, bf16[256,8192]{1,0:T(8,128)(2,1)} %param.12), kind=kOutput, calls=%fused_computation.10 | convolution fusion | flops 2147614720 | bytes 12845056 | tf_op jit(solution)/shard_map/dot_general | solution.py:46
  162.6 1.9 fusion.3
  164.5 4.3 %all-to-all-start.2 = ((bf16[8,256,256]{2,1,0:T(8,128)(2,1)}), bf16[8,256,256]{2,1,0:T(8,128)(2,1)S(1)}, u32[]{:S(2)}, u32[]{:S(2)}) async-start(bf16[8,256,256]{2,1,0:T(8,128)(2,1)} %bitcast.9), calls=%async_computation.2 | async-start | bytes 2097152 | tf_op jit(solution)/shard_map/all_to_all | solution.py:52
  168.7 9.2 %divide_convert_fusion = bf16[4,256,4096]{2,1,0:T(8,128)(2,1)} fusion(f32[256,4096]{1,0:T(8,128)} %broadcast_add_fusion, bf16[4,256,256]{2,1,0:T(8,128)(2,1)S(1)} %copy-done, bf16[4,256,4096]{2,1,0:T(8,128)(2,1)} %param.15), kind=kOutput, calls=%fused_computation | convolution fusion | flops 2155872256 | bytes 21495808 | tf_op jit(solution)/shard_map/qti,qtk->qik/dot_general | solution.py:61
  177.9 6.7 %all-to-all-done.2 = bf16[8,256,256]{2,1,0:T(8,128)(2,1)S(1)} async-done(((bf16[8,256,256]{2,1,0:T(8,128)(2,1)}), bf16[8,256,256]{2,1,0:T(8,128)(2,1)S(1)}, u32[]{:S(2)}, u32[]{:S(2)}) %all-to-all-start.2) | async-done | bytes 1048608 | tf_op jit(solution)/shard_map/all_to_all | solution.py:52
  184.7 1.1 copy-done.2
  185.7 1.4 convert.1
  187.1 90.2 %all-gather.8.cloned.1.call-done = bf16[8,256,4096]{2,1,0:T(8,128)(2,1)} async-done(((bf16[8,256,256]{2,1,0:T(8,128)(2,1)}), bf16[8,256,4096]{2,1,0:T(8,128)(2,1)}) %all-gather.8.cloned.1.call-update) | async-done | bytes 16777232 | tf_op jit(solution)/shard_map/all_gather | solution.py:55
  277.4 24.1 %fusion.6 = f32[2048,1024]{1,0:T(8,128)} fusion(bf16[2048,4096]{1,0:T(8,128)(2,1)} %bitcast.37, bf16[1024,4096]{1,0:T(8,128)(2,1)} %bitcast.38), kind=kOutput, calls=%fused_computation.19 | convolution fusion | flops 17179869184 | bytes 33554432 | tf_op jit(solution)/shard_map/dot_general | solution.py:66
  301.5 10.6 %reshape.106 = f32[2048,4,256]{2,1,0:T(4,128)} reshape(f32[2048,1024]{1,0:T(8,128)} %fusion.6) | data formatting | bytes 16777216 | tf_op jit(solution)/shard_map/reshape | solution.py:69
  312.1 6.3 %multiply_reduce_fusion = f32[2048,4]{1,0:T(8,128)S(1)} fusion(f32[2048,4,256]{2,1,0:T(4,128)} %reshape.106, f32[2048,256]{1,0:T(8,128)S(1)} %convert.1), kind=kLoop, calls=%fused_computation.1 | loop fusion | flops 4186112 | bytes 10518528 | tf_op jit(solution)/shard_map/reduce_sum | solution.py:70
  318.6 22.7 %all-gather.1 = f32[16,4,16]{2,1,0:T(4,128)S(1)} all-gather(f32[1,4,16]{2,1,0:T(4,128)S(1)} %bitcast.31), channel_id=2, replica_groups=mesh['dp'=8,'eig'=16] {'eig'}, dimensions={0}, use_global_device_ids=true | all-gather | bytes 4352 | tf_op jit(solution)/shard_map/all_gather | solution.py:72
  (21 shorter events, 3.8 us)
Async XLA Ops:
  6.5 162.2 %copy-start = (bf16[4,256,256]{2,1,0:T(8,128)(2,1)S(1)}, bf16[4,256,256]{2,1,0:T(8,128)(2,1)}, u32[]{:S(2)}) copy-start(bf16[4,256,256]{2,1,0:T(8,128)(2,1)} %param.14) | copy-start | bytes 1572868
  6.5 76.4 %all-gather.6.cloned.1.call-start = ((), (), s32[]{:S(2)}) async-start(), calls=%async_computation.3 | async-start | bytes 8912896 | tf_op jit(solution)/shard_map/all_gather | solution.py:45
  7.3 148.4 %all-gather.10.cloned.1.call-start = ((), (), s32[]{:S(2)}) async-start(), calls=%async_computation.5 | async-start | bytes 8912896 | tf_op jit(solution)/shard_map/all_gather | solution.py:45
  10.5 9.7 %all-to-all-start = ((s32[1,8,2]{2,0,1:T(1,128)}), s32[1,8,2]{2,0,1:T(1,128)S(1)}, u32[]{:S(2)}, u32[]{:S(2)}) async-start(s32[1,8,2]{2,0,1:T(1,128)} %bitcast), calls=%async_computation | async-start | bytes 8192 | tf_op jit(solution)/shard_map/all_to_all | solution.py:27
  14.9 262.5 %all-gather.8.cloned.1.call-start = ((), (), s32[]{:S(2)}) async-start(), calls=%async_computation.4 | async-start | bytes 17825792 | tf_op jit(solution)/shard_map/all_gather | solution.py:55
  164.5 20.2 %all-to-all-start.2 = ((bf16[8,256,256]{2,1,0:T(8,128)(2,1)}), bf16[8,256,256]{2,1,0:T(8,128)(2,1)S(1)}, u32[]{:S(2)}, u32[]{:S(2)}) async-start(bf16[8,256,256]{2,1,0:T(8,128)(2,1)} %bitcast.9), calls=%async_computation.2 | async-start | bytes 2097152 | tf_op jit(solution)/shard_map/all_to_all | solution.py:52
  184.7 1.1 copy-start.2
  301.5 40.4 %copy-start.1 = (bf16[4,256,256]{2,1,0:T(8,128)(2,1)S(1)}, bf16[4,256,256]{2,1,0:T(8,128)(2,1)}, u32[]{:S(2)}) copy-start(bf16[4,256,256]{2,1,0:T(8,128)(2,1)} %param.14) | copy-start | bytes 1572868
Sparse Core Ops, SparseCore 0:
  9.5 73.4 all-gather.5
  85.1 70.4 all-gather.9
  157.8 119.5 all-gather.7
